TPU v7x, 128 devices: a whole 4x4x4 slice. The times are simulated.
128 devices in a mesh: dp: 4 (over z_lo, core), tensor: 32 (over y, x, z_hi).
Axes of the slice: x: 4, y: 4, z: 4 (z_hi: 2, z_lo: 2; z = z_hi * 2 + z_lo), core: 2. Of those that a mesh axis runs over, the one named last changes fastest.
Arguments:
- stream: bfloat16 [6144, 2560], P(('dp', 'tensor')), may hold values from -26 to 26
- lengths: int32 [4, 6], P('dp'), may hold values from 16 to 768, as said below
- page_table: int32 [384], P('dp'), may hold values from 0 to 383, as said below
- request_prompt: int32 [64], P('dp'), may hold values from 0 to 23
- attn_gain: bfloat16 [2560], replicated, may hold values from 0.099609375 to 1.8984375
- query_gain: bfloat16 [128], replicated, may hold values from 0.5 to 10, as said below
- key_gain: bfloat16 [128], replicated, may hold values from 0.5 to 10, as said below
- mlp_gain: bfloat16 [2560], replicated, may hold values from 0.099609375 to 1.8984375
- w_query: bfloat16 [2560, 4096], P(None, 'tensor'), may hold values from -0.125 to 0.125
- key_value_weight: bfloat16 [2560, 2048], P(None, 'tensor'), may hold values from -0.125 to 0.125
- w_out: bfloat16 [4096, 2560], P('tensor'), may hold values from -0.5 to 0.5
- w_gate: bfloat16 [2560, 9728], P(None, 'tensor'), may hold values from -0.125 to 0.125
- w_up: bfloat16 [2560, 9728], P(None, 'tensor'), may hold values from -0.125 to 0.125
- w_down: bfloat16 [9728, 2560], P('tensor'), may hold values from -0.0625 to 0.0625
Outputs:
- layer_out: bfloat16 [6144, 2560], P(('dp', 'tensor'))
- paged_key_value_cache: bfloat16 [384, 16, 2048], P('dp', None, 'tensor')
- request_state: bfloat16 [64, 2560], P('dp', 'tensor')
Inputs may be any that keep to these rules, and one draw needn't show every extreme that they name: Every length is a multiple of 16; each batch's lengths add up to 1536, and the largest length of each batch is exactly 768. page_table is a permutation of all global slots; slot v belongs to owner v // 96, and each batch writes exactly 24 pages to each owner. `query_gain`: positive gains. `key_gain`: positive gains.
All inputs are finite; a program needn't handle non-finite values.
Results may differ from a plain program's by a relative error of at most 0.02.
The roundings to bfloat16 on the way count: a program that leaves them out, or rounds other values in their place, can miss the bound.
Values may be sent and summed in bfloat16 or wider, within the bound.
No kernel may reach another device: no remote copies, remote signals or barrier semaphores. Data moves between devices by JAX's collectives and lax.ppermute only.
A program may use at most 128 MiB of HBM per device.

v0:
```python
import math
import jax
import jax.numpy as jnp
from jax import lax
from jax.sharding import PartitionSpec as P

KEY_VALUE_HEADS = 8
HEAD_SIZE = 128
PAGE_TOKENS = 16
TENSOR = ("ty", "tx", "tz")
TENSOR_SHAPE = (4, 4, 2)
epsilon = 1e-06
rope_base = 1000000.0


def partner_2(value, axis, bit):
    mask = 2**bit
    pairs = [(source, source ^ mask) for source in range(lax.axis_size(axis))]
    return lax.ppermute(value, axis, pairs)


def scatter_sum(partial, parts):
    pieces = partial.reshape((parts, partial.shape[0] // parts) + partial.shape[1:])
    got = lax.all_to_all(pieces, TENSOR, 0, 0, tiled=True)
    return jnp.sum(got.astype(jnp.float32), axis=0)


def gather_rows(rows):
    rows = lax.all_gather(rows, "tz", axis=0, tiled=True)
    return lax.all_gather(rows, ("ty", "tx"), axis=0, tiled=True)


def row_norm(inputs, gain):
    inputs = inputs.astype(jnp.float32)
    scale = lax.rsqrt(jnp.mean(inputs * inputs, axis=-1, keepdims=True) + epsilon)
    return inputs * scale * gain.astype(jnp.float32)


def rotate(inputs, position):
    half_dim = inputs.shape[-1] // 2
    frequency = rope_base ** (-2.0 * jnp.arange(half_dim, dtype=jnp.float32) / inputs.shape[-1])
    angles = position.astype(jnp.float32)[:, None] * frequency[None, :]
    cosine = jnp.cos(angles)[:, None, :]
    sine_part = jnp.sin(angles)[:, None, :]
    front = inputs[..., :half_dim]
    second = inputs[..., half_dim:]
    return jnp.concatenate(
        [front * cosine - second * sine_part, second * cosine + front * sine_part], axis=-1
    )


def prompt_layout(lengths_row, token_count):
    prompt_ends = jnp.cumsum(lengths_row)
    prompt_starts = prompt_ends - lengths_row
    row_ids = jnp.arange(token_count, dtype=jnp.int32)
    prompt = jnp.sum((row_ids[:, None] >= prompt_ends[None, :]).astype(jnp.int32), axis=1)
    inside = (row_ids[:, None] >= prompt_starts[None, :]) & (
        row_ids[:, None] < prompt_ends[None, :]
    )
    offset = jnp.sum(jnp.where(inside, prompt_starts[None, :], 0), axis=1)
    return (prompt, row_ids - offset, prompt_starts, prompt_ends)


def per_device(
    stream,
    lengths,
    page_table,
    request_prompt,
    attn_gain,
    query_gain,
    key_gain,
    mlp_gain,
    w_query,
    key_value_weight,
    w_out,
    w_gate,
    w_up,
    w_down,
):
    tok_dev = stream.shape[0]
    tensor_element_count = lax.axis_size(TENSOR)
    token_count = tok_dev * tensor_element_count
    my_index = lax.axis_index(TENSOR)
    heads_dev = w_query.shape[1] // HEAD_SIZE
    query_cols = heads_dev * HEAD_SIZE
    prompt, position, prompt_starts, prompt_ends = prompt_layout(lengths[0], token_count)
    portion = gather_rows(row_norm(stream, attn_gain).astype(jnp.bfloat16))
    key_value_group = tensor_element_count // KEY_VALUE_HEADS
    head_weight = key_value_weight
    for bit_id in range(key_value_group.bit_length() - 1):
        partner = partner_2(head_weight, TENSOR, bit_id)
        upper_half = my_index // 2**bit_id % 2
        head_weight = jnp.where(
            upper_half == 1,
            jnp.concatenate([partner, head_weight], axis=1),
            jnp.concatenate([head_weight, partner], axis=1),
        )
    joined = jnp.dot(
        portion, jnp.concatenate([w_query, head_weight], axis=1), preferred_element_type=jnp.float32
    )
    queries = joined[:, :query_cols].reshape(token_count, heads_dev, HEAD_SIZE)
    kv_part = joined[:, query_cols:].astype(jnp.bfloat16)
    key_flat = rotate(row_norm(kv_part[:, None, :HEAD_SIZE], key_gain), position).astype(
        jnp.bfloat16
    )[:, 0, :]
    value_matrix_rows = kv_part[:, HEAD_SIZE:]
    q_rot = rotate(row_norm(queries, query_gain), position).astype(jnp.bfloat16)
    piece_cols = key_value_weight.shape[1]
    head_rows = jnp.concatenate([key_flat, value_matrix_rows], axis=1)
    own_cols = lax.dynamic_slice_in_dim(
        head_rows, my_index % key_value_group * piece_cols, piece_cols, 1
    )
    page_count = token_count // PAGE_TOKENS
    page_rows = own_cols.reshape(page_count, PAGE_TOKENS, piece_cols)
    group_count = lax.axis_size("dp")
    capacity = page_count // group_count
    owners = page_table // page_count
    slot_ids = page_table % page_count
    hits = (owners[:, None] == jnp.arange(group_count, dtype=jnp.int32)[None, :]).astype(jnp.int32)
    order_in = jnp.sum((jnp.cumsum(hits, axis=0) - hits) * hits, axis=1)
    buffer_pos = owners * capacity + order_in
    source = (
        jnp.zeros((page_count,), jnp.int32)
        .at[buffer_pos]
        .set(jnp.arange(page_count, dtype=jnp.int32))
    )
    send_pages = page_rows[source].reshape(group_count, capacity, PAGE_TOKENS, piece_cols)
    send_slots = slot_ids[source].reshape(group_count, capacity)
    got_pages, got_slots = (
        lax.all_to_all(send_pages, "dp", split_axis=0, concat_axis=0, tiled=True),
        lax.all_to_all(send_slots, "dp", split_axis=0, concat_axis=0, tiled=True),
    )
    paged_key_value_cache = (
        jnp.zeros((page_count, PAGE_TOKENS, piece_cols), jnp.bfloat16)
        .at[got_slots.reshape(-1)]
        .set(got_pages.reshape(page_count, PAGE_TOKENS, piece_cols))
    )
    block_rows = min(512, token_count)
    block_total = token_count // block_rows
    score_scale = math.sqrt(HEAD_SIZE)
    all_ids = jnp.arange(token_count, dtype=jnp.int32)
    local_ids = jnp.arange(block_rows, dtype=jnp.int32)

    def dense_block(block_index):
        first_row = block_index * block_rows
        key_count = first_row + block_rows
        key_first = max(0, first_row - 768)
        q_block = q_rot[first_row:key_count]
        q_prompt = prompt[first_row:key_count]
        row_ids = first_row + local_ids
        scores = (
            jnp.einsum(
                "qhd,kd->hqk",
                q_block,
                key_flat[key_first:key_count],
                preferred_element_type=jnp.float32,
            )
            / score_scale
        )
        allowed = (
            (q_prompt[:, None] == prompt[None, key_first:key_count])
            & (row_ids[:, None] >= all_ids[None, key_first:key_count])
        )[None]
        peak = jnp.max(jnp.where(allowed, scores, -jnp.inf), axis=2, keepdims=True)
        weight = jnp.where(allowed, jnp.exp(scores - peak), 0.0)
        total_weight = jnp.sum(weight, axis=2, keepdims=True)
        running = jnp.einsum(
            "hqk,kd->hqd",
            weight.astype(jnp.bfloat16),
            value_matrix_rows[key_first:key_count],
            preferred_element_type=jnp.float32,
        )
        return (running / total_weight).astype(jnp.bfloat16)

    blocks_out = jnp.stack([dense_block(block_index) for block_index in range(block_total)])
    attn = jnp.transpose(blocks_out, (0, 2, 1, 3)).reshape(token_count, query_cols)
    attn_sum = scatter_sum(
        jnp.dot(attn, w_out, preferred_element_type=jnp.float32).astype(jnp.bfloat16),
        tensor_element_count,
    )
    resid = (stream.astype(jnp.float32) + attn_sum).astype(jnp.bfloat16)
    portion = gather_rows(row_norm(resid, mlp_gain).astype(jnp.bfloat16))
    paged_key_value_cache, portion = lax.optimization_barrier((paged_key_value_cache, portion))
    both = jnp.dot(
        portion, jnp.concatenate([w_gate, w_up], axis=1), preferred_element_type=jnp.float32
    )
    gate_rows = both[:, : w_gate.shape[1]]
    upward = both[:, w_gate.shape[1] :]
    hidden = (jax.nn.silu(gate_rows) * upward).astype(jnp.bfloat16)
    width = w_down.shape[1]
    feat = width // tensor_element_count
    nprompt = prompt_ends.shape[0]
    end_pick = ((prompt_ends - 1)[:, None] == all_ids[None, :]).astype(jnp.bfloat16)
    end_hidden = jnp.dot(end_pick, hidden, preferred_element_type=jnp.float32).astype(jnp.bfloat16)
    end_down = jnp.dot(end_hidden, w_down, preferred_element_type=jnp.float32).astype(jnp.bfloat16)
    my_rows = my_index * tok_dev + jnp.arange(tok_dev, dtype=jnp.int32)
    select = ((prompt_ends - 1)[:, None] == my_rows[None, :]).astype(jnp.bfloat16)
    end_resid = jnp.dot(select, resid, preferred_element_type=jnp.float32).astype(jnp.bfloat16)

    def by_feature_block(rows):
        blocks = rows.reshape(nprompt, tensor_element_count, feat)
        return jnp.transpose(blocks, (1, 0, 2)).reshape(tensor_element_count, nprompt * feat)

    extra = jnp.concatenate([by_feature_block(end_down), by_feature_block(end_resid)], axis=1)
    extra_cols = 128
    extra = jnp.pad(extra, ((0, 0), (0, tok_dev * extra_cols - extra.shape[1])))
    wide_weight = jnp.concatenate(
        [w_down, jnp.zeros((w_down.shape[0], extra_cols), w_down.dtype)], axis=1
    )
    down = jnp.dot(hidden, wide_weight, preferred_element_type=jnp.float32).astype(jnp.bfloat16)
    payload = lax.dynamic_update_slice(
        down.reshape(tensor_element_count, tok_dev, width + extra_cols),
        extra.reshape(tensor_element_count, tok_dev, extra_cols),
        (0, 0, width),
    )
    got = lax.all_to_all(payload, TENSOR, 0, 0, tiled=True)
    summed = jnp.sum(got.astype(jnp.float32), axis=0)
    mlp_sum = summed[:, :width]
    layer_out = (resid.astype(jnp.float32) + mlp_sum).astype(jnp.bfloat16)
    tail = summed[:, width:].reshape(-1)
    end_rows = (
        (tail[: nprompt * feat] + tail[nprompt * feat : 2 * nprompt * feat])
        .reshape(nprompt, feat)
        .astype(jnp.bfloat16)
    )
    table = lax.all_gather(end_rows, "dp", axis=0, tiled=True)
    pick = (request_prompt[:, None] == jnp.arange(table.shape[0], dtype=jnp.int32)[None, :]).astype(
        jnp.bfloat16
    )
    request_state = jnp.dot(pick, table, preferred_element_type=jnp.float32).astype(jnp.bfloat16)
    return (layer_out, paged_key_value_cache, request_state)


def solution(mesh):
    placed = (
        P(("dp",) + TENSOR, None),
        P("dp", None),
        P("dp"),
        P("dp"),
        P(),
        P(),
        P(),
        P(),
        P(None, TENSOR),
        P(None, TENSOR),
        P(TENSOR, None),
        P(None, TENSOR),
        P(None, TENSOR),
        P(TENSOR, None),
    )
    dp_size = mesh.shape["dp"]
    fine = jax.sharding.Mesh(mesh.devices.reshape((dp_size,) + TENSOR_SHAPE), ("dp",) + TENSOR)
    return jax.shard_map(
        per_device,
        mesh=fine,
        in_specs=placed,
        out_specs=(P(("dp",) + TENSOR, None), P("dp", None, TENSOR), P("dp", TENSOR)),
        check_vma=False,
    )
```

profile of v0, /device:TPU:27, one launch (start us, length us, event | category | flops | bytes accessed | tf_op | source)
XLA Modules:
  0.0 503.4 jit_solution(10188079126482272437)
XLA Ops:
  7.3 1.2 fusion.62
  9.2 1.1 fusion.64
  10.3 10.0 %all_gather.15 = bf16[96,2560]{1,0:T(8,128)(2,1)} all-gather(bf16[48,2560]{1,0:T(8,128)(2,1)S(1)} %fusion.64), channel_id=1, replica_groups=mesh['dp'=4,'ty'=4,'tx'=4,'tz'=2] {'tz'}, dimensions={0}, use_global_device_ids=true | all-gather | bytes 737280 | tf_op jit(solution)/shard_map/all_gather | solution.py:29
  20.3 2.8 collective-permute-start
  24.8 1.1 copy.29
  25.9 4.2 collective-permute-done
  30.6 22.5 %collective-permute-done.1 = bf16[2560,128]{0,1:T(8,128)(2,1)S(1)} collective-permute-done((bf16[2560,128]{0,1:T(8,128)(2,1)S(1)}, bf16[2560,128]{0,1:T(8,128)(2,1)S(1)}, u32[]{:S(2)}, u32[]{:S(2)}) %collective-permute-start.1) | collective-permute-done | bytes 655392 | tf_op jit(solution)/shard_map/ppermute | solution.py:19
  53.4 41.0 %all-gather.4.cloned.1.call-done = bf16[1536,2560]{1,0:T(8,128)(2,1)} async-done(((bf16[96,2560]{1,0:T(8,128)(2,1)}), bf16[1536,2560]{1,0:T(8,128)(2,1)}) %all-gather.4.cloned.1.call-update) | async-done | bytes 7864336 | tf_op jit(solution)/shard_map/all_gather | solution.py:30
  94.4 5.7 %fusion.129 = (bf16[1536,384]{0,1:T(8,128)(2,1)S(1)}, f32[1536,384]{0,1:T(8,128)S(1)}) fusion(bf16[1536,2560]{1,0:T(8,128)(2,1)} %all-gather.4.cloned.1.call-done, bf16[2560,256]{0,1:T(8,128)(2,1)S(1)} %maximum_select_fusion, bf16[2560,128]{0,1:T(8,128)(2,1)} %copy.29), kind=kOutput, calls=%fused_computation.201 | convolution fusion | flops 3024420864 | bytes 13369344 | tf_op jit(solution)/shard_map/dot_general | solution.py:98
  100.6 1.7 fusion.75
  106.9 1.0 fusion.13
  107.9 1.1 fusion.32
  109.1 5.4 %convolution_convert_fusion.1 = bf16[1536,2560]{1,0:T(8,128)(2,1)} fusion(bf16[1536,128]{1,0:T(8,128)(2,1)S(1)} %bitcast.125, bf16[128,2560]{1,0:T(8,128)(2,1)S(1)} %copy-done), kind=kOutput, calls=%fused_computation.7 | convolution fusion | flops 1010565120 | bytes 8912896 | tf_op jit(solution)/shard_map/dot_general | solution.py:178
  114.4 9.3 %all-to-all-start = ((bf16[32,48,2560]{2,1,0:T(8,128)(2,1)}), bf16[32,48,2560]{2,1,0:T(8,128)(2,1)}, u32[]{:S(2)}, u32[]{:S(2)}) async-start(bf16[32,48,2560]{2,1,0:T(8,128)(2,1)} %bitcast.123), calls=%async_computation | async-start | bytes 15728640 | tf_op jit(solution)/shard_map/all_to_all | solution.py:24
  123.8 121.6 %all-to-all-done = bf16[32,48,2560]{2,1,0:T(8,128)(2,1)} async-done(((bf16[32,48,2560]{2,1,0:T(8,128)(2,1)}), bf16[32,48,2560]{2,1,0:T(8,128)(2,1)}, u32[]{:S(2)}, u32[]{:S(2)}) %all-to-all-start) | async-done | bytes 7864352 | tf_op jit(solution)/shard_map/all_to_all | solution.py:24
  245.4 4.5 convert_reduce_fusion.1
  250.3 8.2 %all_gather.17 = bf16[96,2560]{1,0:T(8,128)(2,1)} all-gather(bf16[48,2560]{1,0:T(8,128)(2,1)S(1)} %fusion.68), channel_id=1, replica_groups=mesh['dp'=4,'ty'=4,'tx'=4,'tz'=2] {'tz'}, dimensions={0}, use_global_device_ids=true | all-gather | bytes 737280 | tf_op jit(solution)/shard_map/all_gather | solution.py:29
  259.9 1.2 gather_fusion
  261.8 5.6 %all-to-all-start.1 = ((s32[4,1,24]{2,1,0:T(1,128)}), s32[4,1,24]{2,1,0:T(1,128)S(1)}, u32[]{:S(2)}, u32[]{:S(2)}) async-start(s32[4,1,24]{2,1,0:T(1,128)} %bitcast.29), calls=%async_computation.1 | async-start | bytes 4096 | tf_op jit(solution)/shard_map/all_to_all | solution.py:131
  267.4 3.0 all-to-all-done.1
  272.8 1.0 reshape.716
  273.8 4.0 all-to-all-start.2
  277.8 4.5 all-to-all-done.2
  282.7 3.5 scatter_fusion
  286.6 39.5 %all-gather.6.cloned.1.call-done = bf16[1536,2560]{1,0:T(8,128)(2,1)} async-done(((bf16[96,2560]{1,0:T(8,128)(2,1)}), bf16[1536,2560]{1,0:T(8,128)(2,1)}) %all-gather.6.cloned.1.call-update) | async-done | bytes 7864336 | tf_op jit(solution)/shard_map/all_gather | solution.py:30
  326.2 7.8 %fusion.1 = f32[1536,608]{0,1:T(8,128)S(1)} fusion(bf16[1536,2560]{1,0:T(8,128)(2,1)} %all-gather.6.cloned.1.call-done, bf16[2560,304]{0,1:T(8,128)(2,1)S(1)} %copy-done.7, bf16[2560,304]{0,1:T(8,128)(2,1)} %param.25), kind=kOutput, calls=%fused_computation.12 | convolution fusion | flops 4787732480 | bytes 14712832 | tf_op jit(solution)/shard_map/dot_general | solution.py:184
  336.3 6.8 %convolution_convert_fusion = bf16[1536,2688]{1,0:T(8,128)(2,1)} fusion(bf16[1536,304]{0,1:T(8,128)(2,1)S(1)} %fusion.12, bf16[304,2560]{1,0:T(8,128)(2,1)S(1)} %copy-done.3), kind=kOutput, calls=%fused_computation.6 | convolution fusion | flops 2514419712 | bytes 10747904 | tf_op jit(solution)/shard_map/dot_general | solution.py:210
  344.4 9.2 %all-to-all-start.3 = ((bf16[32,48,2688]{2,1,0:T(8,128)(2,1)}), bf16[32,48,2688]{2,1,0:T(8,128)(2,1)}, u32[]{:S(2)}, u32[]{:S(2)}) async-start(bf16[32,48,2688]{2,1,0:T(8,128)(2,1)} %constant_dynamic-update-slice_fusion), calls=%async_computation.3 | async-start | bytes 16515072 | tf_op jit(solution)/shard_map/all_to_all | solution.py:216
  353.6 1.1 copy.34
  354.6 128.6 %all-to-all-done.3 = bf16[32,48,2688]{2,1,0:T(8,128)(2,1)} async-done(((bf16[32,48,2688]{2,1,0:T(8,128)(2,1)}), bf16[32,48,2688]{2,1,0:T(8,128)(2,1)}, u32[]{:S(2)}, u32[]{:S(2)}) %all-to-all-start.3) | async-done | bytes 8257568 | tf_op jit(solution)/shard_map/all_to_all | solution.py:216
  483.2 5.0 convert_reduce_fusion
  489.1 6.7 %all-gather = bf16[4,6,80]{2,1,0:T(8,128)(2,1)S(1)} all-gather(bf16[1,6,80]{2,1,0:T(8,128)(2,1)S(1)} %reshape.702), channel_id=1, replica_groups=mesh['dp'=4,'ty'=4,'tx'=4,'tz'=2] {'dp'}, dimensions={0}, use_global_device_ids=true | all-gather | bytes 4800 | tf_op jit(solution)/shard_map/all_gather | solution.py:226
  (105 shorter events, 19.0 us)
Async XLA Ops:
  7.2 101.9 %copy-start = (bf16[128,2560]{1,0:T(8,128)(2,1)S(1)}, bf16[128,2560]{1,0:T(8,128)(2,1)}, u32[]{:S(2)}) copy-start(bf16[128,2560]{1,0:T(8,128)(2,1)} %param.24) | copy-start | bytes 1966084
  7.2 22.9 %copy-start.5 = (bf16[2560,64]{0,1:T(8,128)(2,1)S(1)}, bf16[2560,64]{0,1:T(8,128)(2,1)}, u32[]{:S(2)}) copy-start(bf16[2560,64]{0,1:T(8,128)(2,1)} %param.23) | copy-start | bytes 983044
  7.2 17.5 %copy-start.8 = (bf16[128]{0:T(256)(128)(2,1)S(1)}, bf16[128]{0:T(256)(128)(2,1)}, u32[]{:S(2)}) copy-start(bf16[128]{0:T(256)(128)(2,1)} %param.19) | copy-start | bytes 772
  7.2 17.5 %copy-start.9 = (bf16[128]{0:T(256)(128)(2,1)S(1)}, bf16[128]{0:T(256)(128)(2,1)}, u32[]{:S(2)}) copy-start(bf16[128]{0:T(256)(128)(2,1)} %param.20) | copy-start | bytes 772
  7.2 17.5 %copy-start.4 = (bf16[2560,128]{1,0:T(8,128)(2,1)S(1)}, bf16[2560,128]{1,0:T(8,128)(2,1)}, u32[]{:S(2)}) copy-start(bf16[2560,128]{1,0:T(8,128)(2,1)} %param.22) | copy-start | bytes 1966084
  7.2 87.2 %all-gather.4.cloned.1.call-start = ((), (), s32[]{:S(2)}) async-start(), calls=%async_computation.4 | async-start | bytes 8355840 | tf_op jit(solution)/shard_map/all_gather | solution.py:30
  20.3 9.8 %collective-permute-start = (bf16[2560,64]{0,1:T(8,128)(2,1)}, bf16[2560,64]{0,1:T(8,128)(2,1)S(1)}, u32[]{:S(2)}, u32[]{:S(2)}) collective-permute-start(bf16[2560,64]{0,1:T(8,128)(2,1)} %param.23), channel_id=1, source_target_pairs={{0,1},{1,0},{2,3},{3,2},{4,5},{5,4},{6,7},{7,6},{8,9},{9,8},{10,11... | collective-permute-start | bytes 983048 | tf_op jit(solution)/shard_map/ppermute | solution.py:19
  30.2 22.9 %collective-permute-start.1 = (bf16[2560,128]{0,1:T(8,128)(2,1)S(1)}, bf16[2560,128]{0,1:T(8,128)(2,1)S(1)}, u32[]{:S(2)}, u32[]{:S(2)}) collective-permute-start(bf16[2560,128]{0,1:T(8,128)(2,1)S(1)} %maximum_select_fusion.1), channel_id=1, source_target_pairs={{0,2},{1,3},{2,0},{3,1},{4,6},{5,7},{6,4},{7,5},{8,10},{9,11},{10,... | collective-permute-start | bytes 1966088 | tf_op jit(solution)/shard_map/ppermute | solution.py:19
  114.4 9.4 %copy-start.6 = (bf16[2560]{0:T(1024)(128)(2,1)S(1)}, bf16[2560]{0:T(1024)(128)(2,1)}, u32[]{:S(2)}) copy-start(bf16[2560]{0:T(1024)(128)(2,1)} %param.21) | copy-start | bytes 15364
  114.4 131.0 %all-to-all-start = ((bf16[32,48,2560]{2,1,0:T(8,128)(2,1)}), bf16[32,48,2560]{2,1,0:T(8,128)(2,1)}, u32[]{:S(2)}, u32[]{:S(2)}) async-start(bf16[32,48,2560]{2,1,0:T(8,128)(2,1)} %bitcast.123), calls=%async_computation | async-start | bytes 15728640 | tf_op jit(solution)/shard_map/all_to_all | solution.py:24
  123.7 202.4 %all-gather.6.cloned.1.call-start = ((), (), s32[]{:S(2)}) async-start(), calls=%async_computation.5 | async-start | bytes 8355840 | tf_op jit(solution)/shard_map/all_gather | solution.py:30
  123.8 126.1 %copy-start.2 = (bf16[48,2560]{1,0:T(8,128)(2,1)S(1)}, bf16[48,2560]{1,0:T(8,128)(2,1)}, u32[]{:S(2)}) copy-start(bf16[48,2560]{1,0:T(8,128)(2,1)} %param.14) | copy-start | bytes 737284
  250.0 8.6 %copy-start.10 = (s32[96]{0:T(128)S(1)}, s32[96]{0:T(128)}, u32[]{:S(2)}) copy-start(s32[96]{0:T(128)} %param.16) | copy-start | bytes 1156
  261.8 8.7 %all-to-all-start.1 = ((s32[4,1,24]{2,1,0:T(1,128)}), s32[4,1,24]{2,1,0:T(1,128)S(1)}, u32[]{:S(2)}, u32[]{:S(2)}) async-start(s32[4,1,24]{2,1,0:T(1,128)} %bitcast.29), calls=%async_computation.1 | async-start | bytes 4096 | tf_op jit(solution)/shard_map/all_to_all | solution.py:131
  272.1 54.0 %copy-start.7 = (bf16[2560,304]{0,1:T(8,128)(2,1)S(1)}, bf16[2560,304]{0,1:T(8,128)(2,1)}, u32[]{:S(2)}) copy-start(bf16[2560,304]{0,1:T(8,128)(2,1)} %param.26) | copy-start | bytes 4669444
  273.8 8.5 %all-to-all-start.2 = ((bf16[4,2,12288]{2,1,0:T(2,128)(2,1)}), bf16[4,2,12288]{2,1,0:T(2,128)(2,1)S(1)}, u32[]{:S(2)}, u32[]{:S(2)}) async-start(bf16[4,2,12288]{2,1,0:T(2,128)(2,1)} %reshape.716), calls=%async_computation.2 | async-start | bytes 393216 | tf_op jit(solution)/shard_map/all_to_all | solution.py:130
  334.0 1.4 copy-start.3
  344.4 138.8 %all-to-all-start.3 = ((bf16[32,48,2688]{2,1,0:T(8,128)(2,1)}), bf16[32,48,2688]{2,1,0:T(8,128)(2,1)}, u32[]{:S(2)}, u32[]{:S(2)}) async-start(bf16[32,48,2688]{2,1,0:T(8,128)(2,1)} %constant_dynamic-update-slice_fusion), calls=%async_computation.3 | async-start | bytes 16515072 | tf_op jit(solution)/shard_map/all_to_all | solution.py:216
  354.6 141.1 %copy-start.11 = (s32[16]{0:T(128)S(1)}, s32[16]{0:T(128)}, u32[]{:S(2)}) copy-start(s32[16]{0:T(128)} %param.17) | copy-start | bytes 196
  483.2 13.3 %copy-start.1 = (bf16[128,2560]{1,0:T(8,128)(2,1)S(1)}, bf16[128,2560]{1,0:T(8,128)(2,1)}, u32[]{:S(2)}) copy-start(bf16[128,2560]{1,0:T(8,128)(2,1)} %param.24) | copy-start | bytes 1966084
Sparse Core Ops, SparseCore 0:
  20.4 73.9 all-gather.3
  258.7 67.4 all-gather.5
where the time goes:
time: 504 us; the launch traced here: 503 us
  waiting for transfers between devices  365 us (72%)
  matrix products  32 us (6%)
  starting transfers between devices  31.4 us (6%)
  blocking collectives  24.9 us (5%)
  other arithmetic  22 us (4%)
  between operations  14.6 us (3%)
  local copies, waits for them, and re-layouts  13.6 us (3%)
    all_to_all x1, waiting for transfers between devices, per_device(): got = lax.all_to_all(payload, TENSOR, 0, 0, tiled=True)  129 us
    all_to_all x1, waiting for transfers between devices, scatter_sum(): got = lax.all_to_all(pieces, TENSOR, 0, 0, tiled=True)  122 us
    all_gather x2, waiting for transfers between devices, gather_rows(): return lax.all_gather(rows, ('ty', 'tx'), axis=0, tiled=True)  80.6 us
    ppermute x2, waiting for transfers between devices, partner_2(): return lax.ppermute(value, axis, pairs)  26.7 us
    all_gather x2, blocking collectives, gather_rows(): rows = lax.all_gather(rows, 'tz', axis=0, tiled=True)  18.2 us
  transfers between devices with their start and end apart: 8, of which 8 were waited for; matrix products, arithmetic and copies ran while one was open for 3% of the time, Pallas kernels for 0%

commit v1 on v0

--- a/solution.py
+++ b/solution.py
@@ -27,7 +27,9 @@
 
 def gather_rows(rows):
     rows = lax.all_gather(rows, "tz", axis=0, tiled=True)
-    return lax.all_gather(rows, ("ty", "tx"), axis=0, tiled=True)
+    return jnp.concatenate(
+        lax.all_to_all(jnp.stack([rows] * lax.axis_size(("ty", "tx"))), ("ty", "tx"), 0, 0), axis=0
+    )
 
 
 def row_norm(inputs, gain):

time: 504 us -> 612 us (1.21)
  waiting for transfers between devices: 365 us -> 452 us
  starting transfers between devices: 31.4 us -> 52.8 us
  between operations: 14.6 us -> 1.13 us
  local copies, waits for them, and re-layouts: 13.6 us -> 21.6 us
    all_to_all x0 -> x2, waiting for transfers between devices: none -> 105 us  [gather_rows(): lax.all_to_all(jnp.stack([rows] * lax.axis_size(('ty', 'tx'))), ('ty', 't...]
    ppermute x2, waiting for transfers between devices: 26.7 us -> 119 us  [partner_2(): return lax.ppermute(value, axis, pairs)]
    all_gather x2 -> x0, waiting for transfers between devices: 80.6 us -> none  [gather_rows(): return lax.all_gather(rows, ('ty', 'tx'), axis=0, tiled=True)]
    all_to_all x0 -> x2, starting transfers between devices: none -> 18.1 us  [gather_rows(): lax.all_to_all(jnp.stack([rows] * lax.axis_size(('ty', 'tx'))), ('ty', 't...]
    all_to_all x1, waiting for transfers between devices: 122 us -> 107 us  [scatter_sum(): got = lax.all_to_all(pieces, TENSOR, 0, 0, tiled=True)]
    another operation x0 -> x2, local copies, waits for them, and re-layouts: none -> 7.84 us  [gather_rows(): jnp.stack([rows] * lax.axis_size(('ty', 'tx')))]
    all_to_all x1, waiting for transfers between devices: 129 us -> 121 us  [per_device(): got = lax.all_to_all(payload, TENSOR, 0, 0, tiled=True)]
  transfers between devices with their start and end apart: 8 -> 8, of which waited for: 8 -> 5; matrix products, arithmetic and copies ran while one was open for 3% -> 3% of each run, Pallas kernels for 0% -> 0%
where the time goes in v1:
time: 612 us; the launch traced here: 607 us
  waiting for transfers between devices  452 us (74%)
  starting transfers between devices  52.8 us (9%)
  matrix products  32 us (5%)
  blocking collectives  26.6 us (4%)
  local copies, waits for them, and re-layouts  21.6 us (4%)
  other arithmetic  20.7 us (3%)
    all_to_all x1, waiting for transfers between devices, per_device(): got = lax.all_to_all(payload, TENSOR, 0, 0, tiled=True)  121 us
    ppermute x2, waiting for transfers between devices, partner_2(): return lax.ppermute(value, axis, pairs)  119 us
    all_to_all x1, waiting for transfers between devices, scatter_sum(): got = lax.all_to_all(pieces, TENSOR, 0, 0, tiled=True)  107 us
    all_to_all x2, waiting for transfers between devices, gather_rows(): lax.all_to_all(jnp.stack([rows] * lax.axis_size(('ty', 'tx'))), ('ty', 't...  105 us
    all_gather x2, blocking collectives, gather_rows(): rows = lax.all_gather(rows, 'tz', axis=0, tiled=True)  19.6 us
    all_to_all x2, starting transfers between devices, gather_rows(): lax.all_to_all(jnp.stack([rows] * lax.axis_size(('ty', 'tx'))), ('ty', 't...  18.1 us
    all_to_all x1, starting transfers between devices, per_device(): got = lax.all_to_all(payload, TENSOR, 0, 0, tiled=True)  12.3 us
  transfers between devices with their start and end apart: 8, of which 5 were waited for; matrix products, arithmetic and copies ran while one was open for 3% of the time, Pallas kernels for 0%

profile of v1, /device:TPU:27, one launch (start us, length us, event | category | flops | bytes accessed | tf_op | source)
XLA Modules:
  0.0 606.6 jit_solution(11687497380582514720)
XLA Ops:
  1.4 1.1 fusion.62
  2.5 1.1 fusion.64
  3.6 9.9 %all_gather.9 = bf16[96,2560]{1,0:T(8,128)(2,1)S(1)} all-gather(bf16[48,2560]{1,0:T(8,128)(2,1)S(1)} %fusion.64), channel_id=1, replica_groups=mesh['dp'=4,'ty'=4,'tx'=4,'tz'=2] {'tz'}, dimensions={0}, use_global_device_ids=true | all-gather | bytes 737280 | tf_op jit(solution)/shard_map/all_gather | solution.py:29
  13.5 3.9 stack.12
  17.5 6.7 %all-to-all-start = ((bf16[16,96,2560]{2,1,0:T(8,128)(2,1)}), bf16[16,96,2560]{2,1,0:T(8,128)(2,1)}, u32[]{:S(2)}, u32[]{:S(2)}) async-start(bf16[16,96,2560]{2,1,0:T(8,128)(2,1)} %stack.12), calls=%async_computation | async-start | bytes 15728640 | tf_op jit(solution)/shard_map/all_to_all | solution.py:31
  24.2 2.8 collective-permute-start
  27.3 1.1 copy.29
  28.4 4.9 collective-permute-done
  33.9 114.3 %collective-permute-done.1 = bf16[2560,128]{0,1:T(8,128)(2,1)S(1)} collective-permute-done((bf16[2560,128]{0,1:T(8,128)(2,1)S(1)}, bf16[2560,128]{0,1:T(8,128)(2,1)S(1)}, u32[]{:S(2)}, u32[]{:S(2)}) %collective-permute-start.1) | collective-permute-done | bytes 655392 | tf_op jit(solution)/shard_map/ppermute | solution.py:19
  148.4 5.7 fusion.129
  154.6 1.7 fusion.75
  158.1 1.1 fusion.32
  163.1 5.4 convolution_convert_fusion.1
  168.4 10.2 %all-to-all-start.1 = ((bf16[32,48,2560]{2,1,0:T(8,128)(2,1)}), bf16[32,48,2560]{2,1,0:T(8,128)(2,1)}, u32[]{:S(2)}, u32[]{:S(2)}) async-start(bf16[32,48,2560]{2,1,0:T(8,128)(2,1)} %bitcast.123), calls=%async_computation.1 | async-start | bytes 15728640 | tf_op jit(solution)/shard_map/all_to_all | solution.py:24
  179.1 1.1 scatter_custom_fusion
  180.2 1.2 gather_fusion
  184.2 106.8 %all-to-all-done.1 = bf16[32,48,2560]{2,1,0:T(8,128)(2,1)} async-done(((bf16[32,48,2560]{2,1,0:T(8,128)(2,1)}), bf16[32,48,2560]{2,1,0:T(8,128)(2,1)}, u32[]{:S(2)}, u32[]{:S(2)}) %all-to-all-start.1) | async-done | bytes 7864352 | tf_op jit(solution)/shard_map/all_to_all | solution.py:24
  291.0 5.6 all-to-all-start.2
  296.7 4.6 convert_reduce_fusion.1
  301.5 3.4 all-to-all-start.3
  305.0 9.6 %all_gather.10 = bf16[96,2560]{1,0:T(8,128)(2,1)S(1)} all-gather(bf16[48,2560]{1,0:T(8,128)(2,1)S(1)} %fusion.68), channel_id=1, replica_groups=mesh['dp'=4,'ty'=4,'tx'=4,'tz'=2] {'tz'}, dimensions={0}, use_global_device_ids=true | all-gather | bytes 737280 | tf_op jit(solution)/shard_map/all_gather | solution.py:29
  314.7 3.9 stack.17
  318.6 11.4 %all-to-all-start.4 = ((bf16[16,96,2560]{2,1,0:T(8,128)(2,1)}), bf16[16,96,2560]{2,1,0:T(8,128)(2,1)}, u32[]{:S(2)}, u32[]{:S(2)}) async-start(bf16[16,96,2560]{2,1,0:T(8,128)(2,1)} %stack.17), calls=%async_computation.4 | async-start | bytes 15728640 | tf_op jit(solution)/shard_map/all_to_all | solution.py:31
  331.6 3.4 scatter_fusion
  335.5 105.1 %all-to-all-done.4 = bf16[16,96,2560]{2,1,0:T(8,128)(2,1)} async-done(((bf16[16,96,2560]{2,1,0:T(8,128)(2,1)}), bf16[16,96,2560]{2,1,0:T(8,128)(2,1)}, u32[]{:S(2)}, u32[]{:S(2)}) %all-to-all-start.4) | async-done | bytes 7864352 | tf_op jit(solution)/shard_map/all_to_all | solution.py:31
  440.6 7.8 %fusion.1 = f32[1536,608]{0,1:T(8,128)S(1)} fusion(bf16[1536,2560]{1,0:T(8,128)(2,1)} %bitcast.37, bf16[2560,304]{0,1:T(8,128)(2,1)S(1)} %copy-done.7, bf16[2560,304]{0,1:T(8,128)(2,1)} %param.25), kind=kOutput, calls=%fused_computation.12 | convolution fusion | flops 4787732480 | bytes 14712832 | tf_op jit(solution)/shard_map/dot_general | solution.py:186
  449.8 6.8 %convolution_convert_fusion = bf16[1536,2688]{1,0:T(8,128)(2,1)} fusion(bf16[1536,304]{0,1:T(8,128)(2,1)S(1)} %fusion.12, bf16[304,2560]{1,0:T(8,128)(2,1)S(1)} %copy-done.3), kind=kOutput, calls=%fused_computation.6 | convolution fusion | flops 2514419712 | bytes 10747904 | tf_op jit(solution)/shard_map/dot_general | solution.py:212
  458.8 12.3 %all-to-all-start.5 = ((bf16[32,48,2688]{2,1,0:T(8,128)(2,1)}), bf16[32,48,2688]{2,1,0:T(8,128)(2,1)}, u32[]{:S(2)}, u32[]{:S(2)}) async-start(bf16[32,48,2688]{2,1,0:T(8,128)(2,1)} %constant_dynamic-update-slice_fusion), calls=%async_computation.5 | async-start | bytes 16515072 | tf_op jit(solution)/shard_map/all_to_all | solution.py:218
  471.1 1.1 copy.34
  472.1 120.8 %all-to-all-done.5 = bf16[32,48,2688]{2,1,0:T(8,128)(2,1)} async-done(((bf16[32,48,2688]{2,1,0:T(8,128)(2,1)}), bf16[32,48,2688]{2,1,0:T(8,128)(2,1)}, u32[]{:S(2)}, u32[]{:S(2)}) %all-to-all-start.5) | async-done | bytes 8257568 | tf_op jit(solution)/shard_map/all_to_all | solution.py:218
  592.9 5.0 convert_reduce_fusion
  598.8 7.0 %all-gather = bf16[4,6,80]{2,1,0:T(8,128)(2,1)S(1)} all-gather(bf16[1,6,80]{2,1,0:T(8,128)(2,1)S(1)} %reshape.714), channel_id=1, replica_groups=mesh['dp'=4,'ty'=4,'tx'=4,'tz'=2] {'dp'}, dimensions={0}, use_global_device_ids=true | all-gather | bytes 4800 | tf_op jit(solution)/shard_map/all_gather | solution.py:228
  (107 shorter events, 18.8 us)
Async XLA Ops:
  0.6 162.4 %copy-start = (bf16[128,2560]{1,0:T(8,128)(2,1)S(1)}, bf16[128,2560]{1,0:T(8,128)(2,1)}, u32[]{:S(2)}) copy-start(bf16[128,2560]{1,0:T(8,128)(2,1)} %param.24) | copy-start | bytes 1966084
  17.4 6.8 %copy-start.5 = (bf16[2560,64]{0,1:T(8,128)(2,1)S(1)}, bf16[2560,64]{0,1:T(8,128)(2,1)}, u32[]{:S(2)}) copy-start(bf16[2560,64]{0,1:T(8,128)(2,1)} %param.23) | copy-start | bytes 983044
  17.4 9.5 %copy-start.8 = (s32[1,6]{1,0:T(1,128)S(1)}, s32[1,6]{1,0:T(1,128)}, u32[]{:S(2)}) copy-start(s32[1,6]{1,0:T(1,128)} %param.15) | copy-start | bytes 76
  17.4 9.9 %copy-start.4 = (bf16[2560,128]{1,0:T(8,128)(2,1)S(1)}, bf16[2560,128]{1,0:T(8,128)(2,1)}, u32[]{:S(2)}) copy-start(bf16[2560,128]{1,0:T(8,128)(2,1)} %param.22) | copy-start | bytes 1966084
  17.4 10.9 %copy-start.9 = (bf16[128]{0:T(256)(128)(2,1)S(1)}, bf16[128]{0:T(256)(128)(2,1)}, u32[]{:S(2)}) copy-start(bf16[128]{0:T(256)(128)(2,1)} %param.19) | copy-start | bytes 772
  17.4 10.9 %copy-start.10 = (bf16[128]{0:T(256)(128)(2,1)S(1)}, bf16[128]{0:T(256)(128)(2,1)}, u32[]{:S(2)}) copy-start(bf16[128]{0:T(256)(128)(2,1)} %param.20) | copy-start | bytes 772
  17.5 130.9 %all-to-all-start = ((bf16[16,96,2560]{2,1,0:T(8,128)(2,1)}), bf16[16,96,2560]{2,1,0:T(8,128)(2,1)}, u32[]{:S(2)}, u32[]{:S(2)}) async-start(bf16[16,96,2560]{2,1,0:T(8,128)(2,1)} %stack.12), calls=%async_computation | async-start | bytes 15728640 | tf_op jit(solution)/shard_map/all_to_all | solution.py:31
  24.2 9.1 %collective-permute-start = (bf16[2560,64]{0,1:T(8,128)(2,1)S(1)}, bf16[2560,64]{0,1:T(8,128)(2,1)S(1)}, u32[]{:S(2)}, u32[]{:S(2)}) collective-permute-start(bf16[2560,64]{0,1:T(8,128)(2,1)S(1)} %copy-done.5), channel_id=1, source_target_pairs={{0,1},{1,0},{2,3},{3,2},{4,5},{5,4},{6,7},{7,6},{8,9},{9,8},{10,11... | collective-permute-start | bytes 983048 | tf_op jit(solution)/shard_map/ppermute | solution.py:19
  33.5 114.7 %collective-permute-start.1 = (bf16[2560,128]{0,1:T(8,128)(2,1)S(1)}, bf16[2560,128]{0,1:T(8,128)(2,1)S(1)}, u32[]{:S(2)}, u32[]{:S(2)}) collective-permute-start(bf16[2560,128]{0,1:T(8,128)(2,1)S(1)} %maximum_select_fusion.1), channel_id=1, source_target_pairs={{0,2},{1,3},{2,0},{3,1},{4,6},{5,7},{6,4},{7,5},{8,10},{9,11},{10,... | collective-permute-start | bytes 1966088 | tf_op jit(solution)/shard_map/ppermute | solution.py:19
  168.4 10.2 %copy-start.11 = (s32[96]{0:T(128)S(1)}, s32[96]{0:T(128)}, u32[]{:S(2)}) copy-start(s32[96]{0:T(128)} %param.16) | copy-start | bytes 1156
  168.4 13.7 %copy-start.6 = (bf16[2560]{0:T(1024)(128)(2,1)S(1)}, bf16[2560]{0:T(1024)(128)(2,1)}, u32[]{:S(2)}) copy-start(bf16[2560]{0:T(1024)(128)(2,1)} %param.21) | copy-start | bytes 15364
  168.4 122.6 %all-to-all-start.1 = ((bf16[32,48,2560]{2,1,0:T(8,128)(2,1)}), bf16[32,48,2560]{2,1,0:T(8,128)(2,1)}, u32[]{:S(2)}, u32[]{:S(2)}) async-start(bf16[32,48,2560]{2,1,0:T(8,128)(2,1)} %bitcast.123), calls=%async_computation.1 | async-start | bytes 15728640 | tf_op jit(solution)/shard_map/all_to_all | solution.py:24
  291.0 10.4 %all-to-all-start.2 = ((s32[4,1,24]{2,1,0:T(1,128)}), s32[4,1,24]{2,1,0:T(1,128)S(1)}, u32[]{:S(2)}, u32[]{:S(2)}) async-start(s32[4,1,24]{2,1,0:T(1,128)} %bitcast.30), calls=%async_computation.2 | async-start | bytes 4096 | tf_op jit(solution)/shard_map/all_to_all | solution.py:133
  296.7 4.6 copy-start.2
  301.5 13.2 %all-to-all-start.3 = ((bf16[4,2,12288]{2,1,0:T(2,128)(2,1)}), bf16[4,2,12288]{2,1,0:T(2,128)(2,1)S(1)}, u32[]{:S(2)}, u32[]{:S(2)}) async-start(bf16[4,2,12288]{2,1,0:T(2,128)(2,1)} %reshape.728), calls=%async_computation.3 | async-start | bytes 393216 | tf_op jit(solution)/shard_map/all_to_all | solution.py:132
  318.6 122.0 %all-to-all-start.4 = ((bf16[16,96,2560]{2,1,0:T(8,128)(2,1)}), bf16[16,96,2560]{2,1,0:T(8,128)(2,1)}, u32[]{:S(2)}, u32[]{:S(2)}) async-start(bf16[16,96,2560]{2,1,0:T(8,128)(2,1)} %stack.17), calls=%async_computation.4 | async-start | bytes 15728640 | tf_op jit(solution)/shard_map/all_to_all | solution.py:31
  330.0 110.6 %copy-start.7 = (bf16[2560,304]{0,1:T(8,128)(2,1)S(1)}, bf16[2560,304]{0,1:T(8,128)(2,1)}, u32[]{:S(2)}) copy-start(bf16[2560,304]{0,1:T(8,128)(2,1)} %param.26) | copy-start | bytes 4669444
  448.4 1.4 copy-start.3
  458.8 134.1 %all-to-all-start.5 = ((bf16[32,48,2688]{2,1,0:T(8,128)(2,1)}), bf16[32,48,2688]{2,1,0:T(8,128)(2,1)}, u32[]{:S(2)}, u32[]{:S(2)}) async-start(bf16[32,48,2688]{2,1,0:T(8,128)(2,1)} %constant_dynamic-update-slice_fusion), calls=%async_computation.5 | async-start | bytes 16515072 | tf_op jit(solution)/shard_map/all_to_all | solution.py:218
  472.1 133.7 %copy-start.12 = (s32[16]{0:T(128)S(1)}, s32[16]{0:T(128)}, u32[]{:S(2)}) copy-start(s32[16]{0:T(128)} %param.17) | copy-start | bytes 196
  592.9 13.7 %copy-start.1 = (bf16[128,2560]{1,0:T(8,128)(2,1)S(1)}, bf16[128,2560]{1,0:T(8,128)(2,1)}, u32[]{:S(2)}) copy-start(bf16[128,2560]{1,0:T(8,128)(2,1)} %param.24) | copy-start | bytes 1966084
